TPU v7x, 512 devices: a whole 4x8x8 slice. The times are simulated.
512 devices in a mesh: seg: 16 (over z, x_lo), tok: 32 (over x_hi, y, core).
Axes of the slice: x: 4 (x_hi: 2, x_lo: 2; x = x_hi * 2 + x_lo), y: 8, z: 8, core: 2. Of those that a mesh axis runs over, the one named last changes fastest.
Arguments:
- seg_queries: bfloat16 [16, 4096, 2048], P('seg', 'tok'), may hold values from -8 to 8
- seg_keys: bfloat16 [16, 4096, 512], P('seg', 'tok'), may hold values from -8 to 8
- seg_values: bfloat16 [16, 4096, 512], P('seg', 'tok'), may hold values from -8 to 8
- grad_out: bfloat16 [16, 4096, 2048], P('seg', 'tok'), may hold values from -6 to 6
- mem_init: float32 [256, 1024], P('tok'), may hold values from -6 to 6
- mem_query: bfloat16 [256, 512], P('tok'), may hold values from -8 to 8
- retention: float32 [16, 1024], P('seg'), may hold values from 0 to 1
- seg_len: int32 [16], replicated, may hold values from 1024 to 4096, as said below
- doc_start: int32 [16], replicated, may hold values from 0 to 1, as said below
Outputs:
- attended: bfloat16 [16, 4096, 2048], P('seg', 'tok')
- memory_in: float32 [16, 256, 1024], P('seg', 'tok')
- memory_grad: float32 [16, 256, 1024], P('seg', 'tok')
Inputs may be any that keep to these rules, and one draw needn't show every extreme that they name: `seg_len`: A segment is full unless it is the last one of its document; segment 0 is always full and the last segment is the last one of its document. `doc_start`: segment 0 begins a document and segment 1 never does; any later segment may.
All inputs are finite; a program needn't handle non-finite values.
Results may differ from a plain program's by a relative error of at most 0.009.
Values may be sent and summed in bfloat16 or wider, within the bound.
No kernel may reach another device: no remote copies, remote signals or barrier semaphores. Data moves between devices by JAX's collectives and lax.ppermute only.
A program may use at most 64 MiB of HBM per device.

v0:
```python
import math
import jax
import jax.numpy as jnp
from jax import lax
from jax.sharding import PartitionSpec as P

HD = 128
QH = 16
KVH = 4
loss_scale = 16.0
neg_fill = -1e30
norm_eps = 1e-06


def slot_norm(raw_rows):
    parts = raw_rows.reshape(raw_rows.shape[0], 2 * KVH, HD)
    multiplier = lax.rsqrt(jnp.mean(parts * parts, axis=-1, keepdims=True) + norm_eps)
    return (parts * multiplier).reshape(raw_rows.shape)


def softmax_step(row_top, row_total, scores, allowed):
    scores = jnp.where(allowed, scores, neg_fill)
    new_top = jnp.maximum(row_top, jnp.max(scores, axis=-1))
    weights = jnp.where(allowed, jnp.exp(scores - new_top[..., None]), 0.0)
    multiplier = jnp.exp(row_top - new_top)
    new_total = row_total * multiplier + jnp.sum(weights, axis=-1)
    return (new_top, new_total, weights.astype(jnp.bfloat16), multiplier)


def shards(
    seg_queries, seg_keys, seg_values, grad_out, mem_init, mem_query, retention, seg_len, doc_start
):
    tok_rows = seg_queries.shape[1]
    mem_rows = mem_query.shape[0]
    group_size = QH // KVH
    width_kv = KVH * HD
    seg_count = lax.axis_size("seg")
    seg_index = lax.axis_index("seg")
    tok_index = lax.axis_index("tok")
    length = seg_len[seg_index]
    score_scale = 1.0 / math.sqrt(HD)
    queries = seg_queries[0].reshape(tok_rows, KVH, group_size, HD)
    slot_queries = mem_query.reshape(mem_rows, KVH, HD)
    row_pos = tok_index * tok_rows + jnp.arange(tok_rows)
    kv_piece = lax.all_gather(
        jnp.concatenate([seg_keys[0], seg_values[0]], axis=1), "tok", axis=0, tiled=True
    )
    piece_rows = kv_piece.shape[0]
    key_piece = kv_piece[:, :width_kv].reshape(piece_rows, KVH, HD)
    value_piece = kv_piece[:, width_kv:].reshape(piece_rows, KVH, HD)
    live_keys = jnp.arange(piece_rows) < length
    slot_scores = (
        jnp.einsum("rgd,ugd->gru", slot_queries, key_piece, preferred_element_type=jnp.float32)
        * score_scale
    )
    slot_scores = jnp.where(live_keys, slot_scores, neg_fill)
    slot_top = jnp.max(slot_scores, axis=-1, keepdims=True)
    slot_exp = jnp.where(live_keys, jnp.exp(slot_scores - slot_top), 0.0)
    slot_denom = jnp.transpose(jnp.sum(slot_exp, axis=-1))[..., None]
    slot_weights = slot_exp.astype(jnp.bfloat16)
    slot_keys = jnp.einsum(
        "gru,ugd->rgd", slot_weights, key_piece, preferred_element_type=jnp.float32
    )
    slot_values = jnp.einsum(
        "gru,ugd->rgd", slot_weights, value_piece, preferred_element_type=jnp.float32
    )
    raw_slots = jnp.concatenate(
        [
            (slot_keys / slot_denom).reshape(mem_rows, width_kv),
            (slot_values / slot_denom).reshape(mem_rows, width_kv),
        ],
        axis=1,
    )
    written = slot_norm(raw_slots)
    ret_row = retention[0]
    following = doc_start[jnp.minimum(seg_index + 1, seg_count - 1)].astype(jnp.float32)
    keep_flag = jnp.where(seg_index == seg_count - 1, 1.0, 1.0 - following)
    decay_rate = keep_flag * ret_row
    carried = keep_flag * (1.0 - ret_row) * written + (1.0 - keep_flag) * mem_init
    chain_terms = lax.all_gather(
        jnp.concatenate([carried, decay_rate[None]], axis=0), "seg", axis=0, tiled=False
    )
    all_carried = chain_terms[:, :mem_rows]
    all_decay = chain_terms[:, mem_rows]
    memory_in = mem_init
    for step in range(seg_count - 1):
        following_memory = all_decay[step] * memory_in + all_carried[step]
        memory_in = jnp.where(step < seg_index, following_memory, memory_in)
    block_rows = math.gcd(piece_rows, 512)
    blocks = piece_rows // block_rows
    key_blocks = key_piece.reshape(blocks, block_rows, KVH, HD)
    value_blocks = value_piece.reshape(blocks, block_rows, KVH, HD)
    block_first = block_rows * jnp.arange(blocks)
    starting = (
        jnp.full((KVH, group_size, tok_rows), neg_fill, jnp.float32),
        jnp.zeros((KVH, group_size, tok_rows), jnp.float32),
        jnp.zeros((tok_rows, KVH, group_size, HD), jnp.float32),
    )

    def one_block(inner_state, inputs):
        key_block, value_block, block_start = inputs
        columns = block_start + jnp.arange(block_rows)
        causal = (columns[None, :] <= row_pos[:, None]) & (columns < length)[None, :]
        seg_scores = (
            jnp.einsum("tgjd,ugd->gjtu", queries, key_block, preferred_element_type=jnp.float32)
            * score_scale
        )
        seg_top, seg_total, seg_weights, seg_factor = softmax_step(
            inner_state[0], inner_state[1], seg_scores, causal
        )
        seg_acc = inner_state[2] * jnp.transpose(seg_factor, (2, 0, 1))[..., None] + jnp.einsum(
            "gjtu,ugd->tgjd", seg_weights, value_block, preferred_element_type=jnp.float32
        )
        return ((seg_top, seg_total, seg_acc), None)

    running, _ = lax.scan(one_block, starting, (key_blocks, value_blocks, block_first))
    memory_all = lax.all_gather(memory_in.astype(jnp.bfloat16), "tok", axis=0, tiled=True)
    mem_keys = memory_all[:, :width_kv].reshape(-1, KVH, HD)
    mem_vals = memory_all[:, width_kv:].reshape(-1, KVH, HD)
    mem_scores = (
        jnp.einsum("tgjd,mgd->gjtm", queries, mem_keys, preferred_element_type=jnp.float32)
        * score_scale
    )
    row_top = jnp.maximum(running[0], jnp.max(mem_scores, axis=-1))
    seg_factor = jnp.exp(running[0] - row_top)
    mem_weights = jnp.exp(mem_scores - row_top[..., None])
    row_total = running[1] * seg_factor + jnp.sum(mem_weights, axis=-1)
    weighted = running[2] * jnp.transpose(seg_factor, (2, 0, 1))[..., None] + jnp.einsum(
        "gjtm,mgd->tgjd",
        mem_weights.astype(jnp.bfloat16),
        mem_vals,
        preferred_element_type=jnp.float32,
    )
    att_rows = weighted / jnp.transpose(row_total, (2, 0, 1))[..., None]
    log_total = row_top + jnp.log(row_total)
    attended = att_rows.reshape(1, tok_rows, QH * HD).astype(jnp.bfloat16)
    valid_rows = (row_pos < length).astype(jnp.bfloat16)[:, None]
    cotangent = (grad_out[0] * valid_rows * loss_scale).reshape(tok_rows, KVH, group_size, HD)
    row_delta = jnp.einsum("tgjd,tgjd->gjt", cotangent.astype(jnp.float32), att_rows)
    mem_prob = jnp.exp(mem_scores - log_total[..., None])
    grad_prob = jnp.einsum(
        "tgjd,mgd->gjtm", cotangent, mem_vals, preferred_element_type=jnp.float32
    )
    grad_score = mem_prob * (grad_prob - row_delta[..., None])
    grad_vals = jnp.einsum(
        "gjtm,tgjd->mgd",
        mem_prob.astype(jnp.bfloat16),
        cotangent,
        preferred_element_type=jnp.float32,
    )
    grad_keys = (
        jnp.einsum(
            "gjtm,tgjd->mgd",
            grad_score.astype(jnp.bfloat16),
            queries,
            preferred_element_type=jnp.float32,
        )
        * score_scale
    )
    grad_slots = jnp.concatenate(
        [grad_keys.reshape(-1, width_kv), grad_vals.reshape(-1, width_kv)], axis=1
    )
    local_grad = lax.psum_scatter(grad_slots, "tok", scatter_dimension=0, tiled=True)
    all_local = lax.all_gather(local_grad, "seg", axis=0, tiled=False)
    memory_grad = all_local[seg_count - 1]
    for step in range(seg_count - 2, -1, -1):
        earlier_grad = all_local[step] + all_decay[step] * memory_grad
        memory_grad = jnp.where(step >= seg_index, earlier_grad, memory_grad)
    return (attended, memory_in[None], memory_grad[None])


def solution(mesh):
    placed = (
        P("seg", "tok", None),
        P("seg", "tok", None),
        P("seg", "tok", None),
        P("seg", "tok", None),
        P("tok", None),
        P("tok", None),
        P("seg", None),
        P(),
        P(),
    )
    return jax.shard_map(
        shards,
        mesh=mesh,
        in_specs=placed,
        out_specs=(P("seg", "tok", None), P("seg", "tok", None), P("seg", "tok", None)),
        check_vma=False,
    )
```

profile of v0, /device:TPU:16, one launch (start us, length us, event | category | flops | bytes accessed | tf_op | source)
XLA Modules:
  0.0 526.6 jit_solution(17086343867945131486)
XLA Ops:
  13.7 2.1 copy.163
  18.4 108.9 %all-gather.5.cloned.1.call-done = bf16[4096,1024]{0,1:T(8,128)(2,1)} async-done(((bf16[128,1024]{0,1:T(8,128)(2,1)}), bf16[4096,1024]{0,1:T(8,128)(2,1)}) %all-gather.5.cloned.1.call-update) | async-done | bytes 8388624 | tf_op jit(solution)/shard_map/all_gather | solution.py:45
  127.3 5.9 %fusion.131 = (bf16[4096,512]{0,1:T(8,128)(2,1)}, bf16[4096,512]{0,1:T(8,128)(2,1)}) fusion(bf16[4096,1024]{0,1:T(8,128)(2,1)} %all-gather.5.cloned.1.call-done), kind=kLoop, calls=%fused_computation.186 | loop fusion | bytes 16777216 | tf_op jit(solution)/shard_map/slice | solution.py:49
  133.2 3.1 fusion.134
  136.3 3.5 fusion.45
  141.3 41.0 %all-gather.2 = f32[16,9,1024]{2,1,0:T(8,128)S(1)} all-gather(f32[1,9,1024]{2,1,0:T(8,128)S(1)} %maximum_bitcast_fusion), channel_id=2, replica_groups=mesh['seg'=16,'tok'=32] {'seg'}, dimensions={0}, use_global_device_ids=true | all-gather | bytes 626688 | tf_op jit(solution)/shard_map/all_gather | solution.py:80
  183.1 40.3 %all_gather.21 = bf16[256,1024]{1,0:T(8,128)(2,1)S(1)} all-gather(bf16[8,1024]{1,0:T(8,128)(2,1)S(1)} %get-tuple-element.175), channel_id=1, replica_groups=mesh['seg'=16,'tok'=32] {'tok'}, dimensions={0}, use_global_device_ids=true | all-gather | bytes 540672 | tf_op jit(solution)/shard_map/all_gather | solution.py:117
  224.3 2.0 bitcast_reduce_fusion
  226.3 6.4 %copy.166 = bf16[64,8,8,512]{3,2,1,0:T(8,128)(2,1)} copy(bf16[64,8,8,512]{3,1,2,0:T(8,128)(2,1)} %bitcast.463) | data formatting | bytes 8388608
  232.7 7.9 %copy.118 = bf16[8,512,4,128]{3,1,2,0:T(8,128)(2,1)} copy(bf16[8,512,4,128]{1,0,3,2:T(8,128)(2,1)} %bitcast.464) | data formatting | bytes 8388608
  240.6 4.4 copy.167
  245.1 3.4 copy.120
  248.5 100.9 %while.15 = (s32[]{:T(128)}, f32[4,4,128]{2,1,0:T(4,128)S(1)}, f32[4,4,128]{2,1,0:T(4,128)S(1)}, f32[128,4,4,128]{0,3,2,1:T(8,128)}, s32[8]{0:T(128)S(1)}, /*ind...) while((s32[]{:T(128)}, f32[4,4,128]{2,1,0:T(4,128)S(1)}, ...), condition=%wide.region_3.4_spmd.clone, body=%wide.region_0.3_spmd.clone.sunk | while | flops 551433856 | bytes 33431024 | solution.py:116
  251.3 3.8 fusion.160
  255.1 4.7 fusion.164
  263.6 3.8 fusion.160
  267.4 5.0 fusion.164
  276.3 3.8 fusion.160
  280.1 5.0 fusion.164
  288.9 3.8 fusion.160
  292.7 5.0 fusion.164
  301.6 3.8 fusion.160
  305.4 5.0 fusion.164
  314.2 3.8 fusion.160
  318.0 5.0 fusion.164
  326.9 3.8 fusion.160
  330.7 5.0 fusion.164
  339.5 3.8 fusion.160
  343.3 5.0 fusion.164
  351.3 2.7 fusion.135
  361.9 120.3 %reduce-scatter.2.cloned.1.call-done = f32[8,1024]{1,0:T(8,128)} async-done(((f32[256,1024]{1,0:T(8,128)}), f32[8,1024]{1,0:T(8,128)}) %reduce-scatter.2.cloned.1.call-update) | async-done | bytes 32784 | tf_op jit(solution)/shard_map/reduce_scatter | solution.py:163
  482.2 36.8 %all-gather.1 = f32[128,1024]{1,0:T(8,128)S(1)} all-gather(f32[8,1024]{1,0:T(8,128)} %reduce-scatter.2.cloned.1.call-done), channel_id=3, replica_groups=mesh['seg'=16,'tok'=32] {'seg'}, dimensions={0}, use_global_device_ids=true | all-gather | bytes 557056 | tf_op jit(solution)/shard_map/all_gather | solution.py:164
  (189 shorter events, 52.6 us)
Async XLA Ops:
  7.2 126.1 %copy-start = (bf16[8,512]{1,0:T(8,128)(2,1)S(1)}, bf16[8,512]{1,0:T(8,128)(2,1)}, u32[]{:S(2)}) copy-start(bf16[8,512]{1,0:T(8,128)(2,1)} %param.16) | copy-start | bytes 24580
  7.2 8.6 %copy-start.15 = (s32[16]{0:T(128)S(1)}, s32[16]{0:T(128)}, u32[]{:S(2)}) copy-start(s32[16]{0:T(128)} %param.18) | copy-start | bytes 196
  7.2 11.2 %copy-start.13 = (f32[1,1024]{1,0:T(1,128)S(1)}, f32[1,1024]{1,0:T(1,128)}, u32[]{:S(2)}) copy-start(f32[1,1024]{1,0:T(1,128)} %param.17) | copy-start | bytes 12292
  7.2 120.1 %all-gather.5.cloned.1.call-start = ((), (), s32[]{:S(2)}) async-start(), calls=%async_computation.1 | async-start | bytes 8650752 | tf_op jit(solution)/shard_map/all_gather | solution.py:45
  10.1 472.2 %reduce-scatter.2.cloned.1.call-start = ((), (), s32[]{:S(2)}) async-start(), calls=%async_computation.2 | async-start | bytes 1081344 | tf_op jit(solution)/shard_map/reduce_scatter | solution.py:163
  136.3 3.5 copy-start.2
  136.3 4.8 copy-start.6
  182.3 0.8 copy-start.7
  182.3 0.8 copy-start.9
  255.1 4.7 copy-start.1
  259.8 1.1 copy-start.17
  267.4 5.0 copy-start.1
  272.4 1.1 copy-start.17
  280.1 5.0 copy-start.1
  285.0 1.1 copy-start.17
  292.7 5.0 copy-start.1
  297.7 1.1 copy-start.17
  305.4 5.0 copy-start.1
  310.3 1.1 copy-start.17
  318.0 5.0 copy-start.1
  323.0 1.1 copy-start.17
  330.7 5.0 copy-start.1
  335.6 1.1 copy-start.17
  343.3 5.0 copy-start.1
  348.3 1.1 copy-start.17
  349.4 4.6 copy-start.3
  349.4 4.6 copy-start.14
  351.2 4.2 copy-start.5
  357.2 3.7 copy-start.4
  357.2 161.9 %copy-start.8 = (f32[1,1,1024]{2,1,0:T(1,128)S(1)}, f32[1,1,1024]{2,1,0:T(1,128)}, u32[]{:S(2)}) copy-start(f32[1,1,1024]{2,1,0:T(1,128)} %copy-done.7) | copy-start | bytes 12292
  357.2 161.9 %copy-start.10 = (f32[1,1,1024]{2,1,0:T(1,128)S(1)}, f32[1,1,1024]{2,1,0:T(1,128)}, u32[]{:S(2)}) copy-start(f32[1,1,1024]{2,1,0:T(1,128)} %copy-done.9) | copy-start | bytes 12292
  357.2 161.9 %copy-start.12 = (f32[1,1,1024]{2,1,0:T(1,128)S(1)}, f32[1,1,1024]{2,1,0:T(1,128)}, u32[]{:S(2)}) copy-start(f32[1,1,1024]{2,1,0:T(1,128)} %copy-done.11) | copy-start | bytes 12292
  (9 other events, 5.6 us)
Sparse Core Ops, SparseCore 0:
  11.7 115.5 all-gather.4
  360.9 121.2 reduce-scatter.1
where the time goes:
time: 528 us; the launch traced here: 527 us
  waiting for transfers between devices  229 us (43%)
  blocking collectives  118 us (22%)
  matrix products  85 us (16%)
  local copies, waits for them, and re-layouts  45.9 us (9%)
  other arithmetic  32.6 us (6%)
  between operations  15 us (3%)
    reduce_scatter x1, waiting for transfers between devices, shards(): lax.psum_scatter(grad_slots, 'tok', scatter_dimension=0, tiled=True)  120 us
    all_gather x1, waiting for transfers between devices, shards(): lax.all_gather(jnp.concatenate([seg_keys[0], seg_values[0]], axis=1), 'to...  109 us
    all_gather x1, blocking collectives, shards(): lax.all_gather(jnp.concatenate([carried, decay_rate[None]], axis=0), 'seg...  41 us
    all_gather x1, blocking collectives, shards(): lax.all_gather(memory_in.astype(jnp.bfloat16), 'tok', axis=0, tiled=True)  40.3 us
    dot_general x8, matrix products, one_block(): jnp.einsum('gjtu,ugd->tgjd', seg_weights, value_block, preferred_element_...  39.5 us
    all_gather x1, blocking collectives, shards(): all_local = lax.all_gather(local_grad, 'seg', axis=0, tiled=False)  36.8 us
    dot_general x8, matrix products, one_block(): jnp.einsum('tgjd,ugd->gjtu', queries, key_block, preferred_element_type=j...  30 us
    unnamed x40, local copies, waits for them, and re-layouts  27.7 us
  transfers between devices with their start and end apart: 2, of which 2 were waited for; matrix products, arithmetic and copies ran while one was open for 2% of the time, Pallas kernels for 0%

commit v1 on v0

--- a/solution.py
+++ b/solution.py
@@ -114,7 +114,12 @@
         return ((seg_top, seg_total, seg_acc), None)
 
     running, _ = lax.scan(one_block, starting, (key_blocks, value_blocks, block_first))
-    memory_all = lax.all_gather(memory_in.astype(jnp.bfloat16), "tok", axis=0, tiled=True)
+    memory_all = jnp.concatenate(
+        lax.all_to_all(
+            jnp.stack([memory_in.astype(jnp.bfloat16)] * lax.axis_size("tok")), "tok", 0, 0
+        ),
+        axis=0,
+    )
     mem_keys = memory_all[:, :width_kv].reshape(-1, KVH, HD)
     mem_vals = memory_all[:, width_kv:].reshape(-1, KVH, HD)
     mem_scores = (

time: 528 us -> 496 us (0.939)
  blocking collectives: 118 us -> 77.8 us
  starting transfers between devices: 0.08 us -> 9.19 us
    all_gather x1 -> x0, blocking collectives: 40.3 us -> none  [shards(): lax.all_gather(memory_in.astype(jnp.bfloat16), 'tok', axis=0, tiled=True)]
    all_to_all x0 -> x1, starting transfers between devices: none -> 9.11 us  [shards(): lax.all_to_all(jnp.stack([memory_in.astype(jnp.bfloat16)] * lax.axis_size...]
    unnamed x40 -> x23, local copies, waits for them, and re-layouts: 27.7 us -> 26.9 us
  transfers between devices with their start and end apart: 2 -> 3, of which waited for: 2 -> 2; matrix products, arithmetic and copies ran while one was open for 2% -> 26% of each run, Pallas kernels for 0% -> 0%
where the time goes in v1:
time: 496 us; the launch traced here: 494 us
  waiting for transfers between devices  231 us (47%)
  matrix products  84.3 us (17%)
  blocking collectives  77.8 us (16%)
  local copies, waits for them, and re-layouts  45.9 us (9%)
  other arithmetic  30.6 us (6%)
  between operations  15 us (3%)
  starting transfers between devices  9.19 us (2%)
    reduce_scatter x1, waiting for transfers between devices, shards(): lax.psum_scatter(grad_slots, 'tok', scatter_dimension=0, tiled=True)  121 us
    all_gather x1, waiting for transfers between devices, shards(): lax.all_gather(jnp.concatenate([seg_keys[0], seg_values[0]], axis=1), 'to...  110 us
    all_gather x1, blocking collectives, shards(): lax.all_gather(jnp.concatenate([carried, decay_rate[None]], axis=0), 'seg...  41 us
    dot_general x8, matrix products, one_block(): jnp.einsum('gjtu,ugd->tgjd', seg_weights, value_block, preferred_element_...  39.4 us
    all_gather x1, blocking collectives, shards(): all_local = lax.all_gather(local_grad, 'seg', axis=0, tiled=False)  36.8 us
    dot_general x8, matrix products, one_block(): jnp.einsum('tgjd,ugd->gjtu', queries, key_block, preferred_element_type=j...  29.9 us
    unnamed x23, local copies, waits for them, and re-layouts  26.9 us
    lt x8, other arithmetic, one_block(): columns < length  10.1 us
  transfers between devices with their start and end apart: 3, of which 2 were waited for; matrix products, arithmetic and copies ran while one was open for 26% of the time, Pallas kernels for 0%

profile of v1, /device:TPU:16, one launch (start us, length us, event | category | flops | bytes accessed | tf_op | source)
XLA Modules:
  0.0 494.4 jit_solution(15992602428137717392)
XLA Ops:
  16.9 110.4 %all-gather.5.cloned.1.call-done = bf16[4096,1024]{0,1:T(8,128)(2,1)} async-done(((bf16[128,1024]{0,1:T(8,128)(2,1)}), bf16[4096,1024]{0,1:T(8,128)(2,1)}) %all-gather.5.cloned.1.call-update) | async-done | bytes 8388624 | tf_op jit(solution)/shard_map/all_gather | solution.py:45
  127.3 5.9 %fusion.131 = (bf16[4096,512]{0,1:T(8,128)(2,1)}, bf16[4096,512]{0,1:T(8,128)(2,1)}) fusion(bf16[4096,1024]{0,1:T(8,128)(2,1)} %all-gather.5.cloned.1.call-done), kind=kLoop, calls=%fused_computation.186 | loop fusion | bytes 16777216 | tf_op jit(solution)/shard_map/slice | solution.py:49
  133.2 3.1 fusion.134
  136.3 3.5 fusion.45
  141.2 41.0 %all-gather.2 = f32[16,9,1024]{2,1,0:T(8,128)S(1)} all-gather(f32[1,9,1024]{2,1,0:T(8,128)S(1)} %maximum_bitcast_fusion), channel_id=2, replica_groups=mesh['seg'=16,'tok'=32] {'seg'}, dimensions={0}, use_global_device_ids=true | all-gather | bytes 626688 | tf_op jit(solution)/shard_map/all_gather | solution.py:80
  183.8 9.1 %all-to-all-start = ((bf16[32,8,1024]{2,1,0:T(8,128)(2,1)}), bf16[32,8,1024]{2,1,0:T(8,128)(2,1)S(1)}, u32[]{:S(2)}, u32[]{:S(2)}) async-start(bf16[32,8,1024]{2,1,0:T(8,128)(2,1)} %stack.2), calls=%async_computation | async-start | bytes 1048576 | tf_op jit(solution)/shard_map/all_to_all | solution.py:118
  193.0 6.4 %copy.94 = bf16[64,8,8,512]{3,2,1,0:T(8,128)(2,1)} copy(bf16[64,8,8,512]{3,1,2,0:T(8,128)(2,1)} %bitcast.464) | data formatting | bytes 8388608
  199.4 7.9 %copy.47 = bf16[8,512,4,128]{3,1,2,0:T(8,128)(2,1)} copy(bf16[8,512,4,128]{1,0,3,2:T(8,128)(2,1)} %bitcast.465) | data formatting | bytes 8388608
  207.3 4.4 copy.95
  211.7 3.4 copy.49
  215.2 100.0 %while.15 = (s32[]{:T(128)}, f32[4,4,128]{2,1,0:T(4,128)S(1)}, f32[4,4,128]{2,1,0:T(4,128)S(1)}, f32[128,4,4,128]{0,3,2,1:T(8,128)}, s32[8]{0:T(128)S(1)}, /*ind...) while((s32[]{:T(128)}, f32[4,4,128]{2,1,0:T(4,128)S(1)}, ...), condition=%wide.region_3.4_spmd.clone, body=%wide.region_0.3_spmd.clone.sunk | while | flops 551433856 | bytes 33430712 | solution.py:116
  217.9 3.7 fusion.160
  221.6 4.7 fusion.164
  230.1 3.7 fusion.160
  233.9 5.0 %fusion.164 = f32[128,4,4,128]{0,3,2,1:T(8,128)} fusion(f32[4,512,128,4]{2,1,3,0:T(8,128)} %get-tuple-element.251, f32[4,4,128]{2,1,0:T(4,128)S(1)} %get-tuple-element.278, pred[128,512]{0,1:T(8,128)(4,1)S(1)} %compare_and_fusion.2, f32[128,4,4,128]{0,3,2,1:T(8,128)} %get-tuple-element.268, bf16[8,512,4,128]{1,3,2,0:T(8,128)(2,1)} %get-tuple-element.285, ...), kind=kOutput, calls=%fused_computation.9.clone.1 | convolution fusion | flops 274464768 | bytes 6898177 | tf_op jit(solution)/shard_map/while/body/eval_jaxpr/gjtu,ugd->tgjd/dot_general | solution.py:111
  242.6 3.7 fusion.160
  246.4 5.0 %fusion.164 = f32[128,4,4,128]{0,3,2,1:T(8,128)} fusion(f32[4,512,128,4]{2,1,3,0:T(8,128)} %get-tuple-element.251, f32[4,4,128]{2,1,0:T(4,128)S(1)} %get-tuple-element.278, pred[128,512]{0,1:T(8,128)(4,1)S(1)} %compare_and_fusion.2, f32[128,4,4,128]{0,3,2,1:T(8,128)} %get-tuple-element.268, bf16[8,512,4,128]{1,3,2,0:T(8,128)(2,1)} %get-tuple-element.285, ...), kind=kOutput, calls=%fused_computation.9.clone.1 | convolution fusion | flops 274464768 | bytes 6898177 | tf_op jit(solution)/shard_map/while/body/eval_jaxpr/gjtu,ugd->tgjd/dot_general | solution.py:111
  255.2 3.7 fusion.160
  259.0 5.0 %fusion.164 = f32[128,4,4,128]{0,3,2,1:T(8,128)} fusion(f32[4,512,128,4]{2,1,3,0:T(8,128)} %get-tuple-element.251, f32[4,4,128]{2,1,0:T(4,128)S(1)} %get-tuple-element.278, pred[128,512]{0,1:T(8,128)(4,1)S(1)} %compare_and_fusion.2, f32[128,4,4,128]{0,3,2,1:T(8,128)} %get-tuple-element.268, bf16[8,512,4,128]{1,3,2,0:T(8,128)(2,1)} %get-tuple-element.285, ...), kind=kOutput, calls=%fused_computation.9.clone.1 | convolution fusion | flops 274464768 | bytes 6898177 | tf_op jit(solution)/shard_map/while/body/eval_jaxpr/gjtu,ugd->tgjd/dot_general | solution.py:111
  267.7 3.7 fusion.160
  271.5 5.0 %fusion.164 = f32[128,4,4,128]{0,3,2,1:T(8,128)} fusion(f32[4,512,128,4]{2,1,3,0:T(8,128)} %get-tuple-element.251, f32[4,4,128]{2,1,0:T(4,128)S(1)} %get-tuple-element.278, pred[128,512]{0,1:T(8,128)(4,1)S(1)} %compare_and_fusion.2, f32[128,4,4,128]{0,3,2,1:T(8,128)} %get-tuple-element.268, bf16[8,512,4,128]{1,3,2,0:T(8,128)(2,1)} %get-tuple-element.285, ...), kind=kOutput, calls=%fused_computation.9.clone.1 | convolution fusion | flops 274464768 | bytes 6898177 | tf_op jit(solution)/shard_map/while/body/eval_jaxpr/gjtu,ugd->tgjd/dot_general | solution.py:111
  280.3 3.7 fusion.160
  284.0 5.0 %fusion.164 = f32[128,4,4,128]{0,3,2,1:T(8,128)} fusion(f32[4,512,128,4]{2,1,3,0:T(8,128)} %get-tuple-element.251, f32[4,4,128]{2,1,0:T(4,128)S(1)} %get-tuple-element.278, pred[128,512]{0,1:T(8,128)(4,1)S(1)} %compare_and_fusion.2, f32[128,4,4,128]{0,3,2,1:T(8,128)} %get-tuple-element.268, bf16[8,512,4,128]{1,3,2,0:T(8,128)(2,1)} %get-tuple-element.285, ...), kind=kOutput, calls=%fused_computation.9.clone.1 | convolution fusion | flops 274464768 | bytes 6898177 | tf_op jit(solution)/shard_map/while/body/eval_jaxpr/gjtu,ugd->tgjd/dot_general | solution.py:111
  292.8 3.7 fusion.160
  296.6 5.0 %fusion.164 = f32[128,4,4,128]{0,3,2,1:T(8,128)} fusion(f32[4,512,128,4]{2,1,3,0:T(8,128)} %get-tuple-element.251, f32[4,4,128]{2,1,0:T(4,128)S(1)} %get-tuple-element.278, pred[128,512]{0,1:T(8,128)(4,1)S(1)} %compare_and_fusion.2, f32[128,4,4,128]{0,3,2,1:T(8,128)} %get-tuple-element.268, bf16[8,512,4,128]{1,3,2,0:T(8,128)(2,1)} %get-tuple-element.285, ...), kind=kOutput, calls=%fused_computation.9.clone.1 | convolution fusion | flops 274464768 | bytes 6898177 | tf_op jit(solution)/shard_map/while/body/eval_jaxpr/gjtu,ugd->tgjd/dot_general | solution.py:111
  305.3 3.7 fusion.160
  309.1 5.0 %fusion.164 = f32[128,4,4,128]{0,3,2,1:T(8,128)} fusion(f32[4,512,128,4]{2,1,3,0:T(8,128)} %get-tuple-element.251, f32[4,4,128]{2,1,0:T(4,128)S(1)} %get-tuple-element.278, pred[128,512]{0,1:T(8,128)(4,1)S(1)} %compare_and_fusion.2, f32[128,4,4,128]{0,3,2,1:T(8,128)} %get-tuple-element.268, bf16[8,512,4,128]{1,3,2,0:T(8,128)(2,1)} %get-tuple-element.285, ...), kind=kOutput, calls=%fused_computation.9.clone.1 | convolution fusion | flops 274464768 | bytes 6898177 | tf_op jit(solution)/shard_map/while/body/eval_jaxpr/gjtu,ugd->tgjd/dot_general | solution.py:111
  316.1 1.4 bitcast_reduce_fusion
  318.7 2.7 fusion.135
  322.9 1.7 fusion.43
  329.3 120.7 %reduce-scatter.2.cloned.1.call-done = f32[8,1024]{1,0:T(8,128)} async-done(((f32[256,1024]{1,0:T(8,128)}), f32[8,1024]{1,0:T(8,128)}) %reduce-scatter.2.cloned.1.call-update) | async-done | bytes 32784 | tf_op jit(solution)/shard_map/reduce_scatter | solution.py:168
  450.0 36.8 %all-gather.1 = f32[128,1024]{1,0:T(8,128)S(1)} all-gather(f32[8,1024]{1,0:T(8,128)} %reduce-scatter.2.cloned.1.call-done), channel_id=3, replica_groups=mesh['seg'=16,'tok'=32] {'seg'}, dimensions={0}, use_global_device_ids=true | all-gather | bytes 557056 | tf_op jit(solution)/shard_map/all_gather | solution.py:169
  (143 shorter events, 51.0 us)
Async XLA Ops:
  7.2 126.0 %copy-start = (bf16[8,512]{1,0:T(8,128)(2,1)S(1)}, bf16[8,512]{1,0:T(8,128)(2,1)}, u32[]{:S(2)}) copy-start(bf16[8,512]{1,0:T(8,128)(2,1)} %param.16) | copy-start | bytes 24580
  7.2 7.8 %copy-start.7 = (s32[16]{0:T(128)S(1)}, s32[16]{0:T(128)}, u32[]{:S(2)}) copy-start(s32[16]{0:T(128)} %param.18) | copy-start | bytes 196
  7.2 9.7 %copy-start.6 = (f32[1,1024]{1,0:T(1,128)S(1)}, f32[1,1024]{1,0:T(1,128)}, u32[]{:S(2)}) copy-start(f32[1,1024]{1,0:T(1,128)} %param.17) | copy-start | bytes 12292
  7.2 120.1 %all-gather.5.cloned.1.call-start = ((), (), s32[]{:S(2)}) async-start(), calls=%async_computation.2 | async-start | bytes 8650752 | tf_op jit(solution)/shard_map/all_gather | solution.py:45
  136.3 3.5 copy-start.2
  136.3 4.8 copy-start.5
  183.8 131.3 %all-to-all-start = ((bf16[32,8,1024]{2,1,0:T(8,128)(2,1)}), bf16[32,8,1024]{2,1,0:T(8,128)(2,1)S(1)}, u32[]{:S(2)}, u32[]{:S(2)}) async-start(bf16[32,8,1024]{2,1,0:T(8,128)(2,1)} %stack.2), calls=%async_computation | async-start | bytes 1048576 | tf_op jit(solution)/shard_map/all_to_all | solution.py:118
  193.0 257.0 %reduce-scatter.2.cloned.1.call-start = ((), (), s32[]{:S(2)}) async-start(), calls=%async_computation.3 | async-start | bytes 1081344 | tf_op jit(solution)/shard_map/reduce_scatter | solution.py:168
  221.6 4.7 copy-start.1
  233.9 5.0 %copy-start.1 = (f32[4,512,128,4]{2,1,3,0:T(8,128)S(1)}, f32[4,512,128,4]{2,1,3,0:T(8,128)}, u32[]{:S(2)}) copy-start(f32[4,512,128,4]{2,1,3,0:T(8,128)} %get-tuple-element.251) | copy-start | bytes 12582916 | tf_op jit(solution)/shard_map/while
  246.4 5.0 %copy-start.1 = (f32[4,512,128,4]{2,1,3,0:T(8,128)S(1)}, f32[4,512,128,4]{2,1,3,0:T(8,128)}, u32[]{:S(2)}) copy-start(f32[4,512,128,4]{2,1,3,0:T(8,128)} %get-tuple-element.251) | copy-start | bytes 12582916 | tf_op jit(solution)/shard_map/while
  258.9 5.0 %copy-start.1 = (f32[4,512,128,4]{2,1,3,0:T(8,128)S(1)}, f32[4,512,128,4]{2,1,3,0:T(8,128)}, u32[]{:S(2)}) copy-start(f32[4,512,128,4]{2,1,3,0:T(8,128)} %get-tuple-element.251) | copy-start | bytes 12582916 | tf_op jit(solution)/shard_map/while
  271.5 5.0 %copy-start.1 = (f32[4,512,128,4]{2,1,3,0:T(8,128)S(1)}, f32[4,512,128,4]{2,1,3,0:T(8,128)}, u32[]{:S(2)}) copy-start(f32[4,512,128,4]{2,1,3,0:T(8,128)} %get-tuple-element.251) | copy-start | bytes 12582916 | tf_op jit(solution)/shard_map/while
  284.0 5.0 %copy-start.1 = (f32[4,512,128,4]{2,1,3,0:T(8,128)S(1)}, f32[4,512,128,4]{2,1,3,0:T(8,128)}, u32[]{:S(2)}) copy-start(f32[4,512,128,4]{2,1,3,0:T(8,128)} %get-tuple-element.251) | copy-start | bytes 12582916 | tf_op jit(solution)/shard_map/while
  296.6 5.0 %copy-start.1 = (f32[4,512,128,4]{2,1,3,0:T(8,128)S(1)}, f32[4,512,128,4]{2,1,3,0:T(8,128)}, u32[]{:S(2)}) copy-start(f32[4,512,128,4]{2,1,3,0:T(8,128)} %get-tuple-element.251) | copy-start | bytes 12582916 | tf_op jit(solution)/shard_map/while
  309.1 5.0 %copy-start.1 = (f32[4,512,128,4]{2,1,3,0:T(8,128)S(1)}, f32[4,512,128,4]{2,1,3,0:T(8,128)}, u32[]{:S(2)}) copy-start(f32[4,512,128,4]{2,1,3,0:T(8,128)} %get-tuple-element.251) | copy-start | bytes 12582916 | tf_op jit(solution)/shard_map/while
  318.7 4.2 copy-start.4
  324.6 3.7 copy-start.3
Sparse Core Ops, SparseCore 0:
  11.7 115.5 all-gather.4
  328.4 121.6 reduce-scatter.1
